TPU v7x, 256 devices: a whole 4x4x8 slice. The times are simulated.
256 devices in a mesh: req: 4 (over x), seq: 8 (over z_lo, y), tp: 8 (over z_hi, core).
Axes of the slice: x: 4, y: 4, z: 8 (z_hi: 4, z_lo: 2; z = z_hi * 2 + z_lo), core: 2. Of those that a mesh axis runs over, the one named last changes fastest.
Arguments:
- img_hidden: bfloat16 [16384, 3072], P(('req', 'seq'), 'tp'), parts along dimension 0, may hold values from -6 to 6
- txt_hidden: bfloat16 [2048, 3072], P(('req', 'seq'), 'tp'), parts along dimension 0, may hold values from -6 to 6
- img_mod: bfloat16 [12, 3072], P('req'), parts along dimension 0, may hold values from -3 to 3
- txt_mod: bfloat16 [12, 3072], P('req'), parts along dimension 0, may hold values from -3 to 3
- img_qkv: bfloat16 [3072, 3, 3072], P('seq', None, 'tp')
- txt_qkv: bfloat16 [3072, 3, 3072], P('seq', None, 'tp'), may hold values from -0.109375 to 0.109375
- qk_gains: float32 [4, 128], replicated, may hold values from 0.5 to 4.5, as said below
- img_out_w: bfloat16 [3072, 3072], P('tp', 'seq'), may hold values from -0.109375 to 0.109375
- txt_out_w: bfloat16 [3072, 3072], P('tp', 'seq'), may hold values from -0.109375 to 0.109375
- final_mod: bfloat16 [8, 3072], P('req'), parts along dimension 0, may hold values from -3 to 3
- final_w: bfloat16 [3072, 64], P('tp'), may hold values from -0.109375 to 0.109375
- conv_w: bfloat16 [3, 3, 64, 64], replicated, may hold values from -0.25 to 0.25
- latent: float32 [256, 4096], P(('req', 'seq'), 'tp'), parts along dimension 0, may hold values from -6 to 6
- text_len: int32 [4], P('req'), parts along dimension 0, may hold values from 1 to 512
- step_index: int32 [4], P('req'), parts along dimension 0, may hold values from 0 to 27
Outputs:
- img_next: bfloat16 [16384, 3072], P(('req', 'seq'), 'tp'), parts along dimension 0
- txt_next: bfloat16 [2048, 3072], P(('req', 'seq'), 'tp'), parts along dimension 0
- velocity: float32 [256, 4096], P(('req', 'seq'), 'tp'), parts along dimension 0
- latent_next: float32 [256, 4096], P(('req', 'seq'), 'tp'), parts along dimension 0
- denoised: float32 [256, 4096], P(('req', 'seq'), 'tp'), parts along dimension 0
There are 4 independent parts, one for each index of `req`. A program takes and returns all parts, laid end to end along the dimension named above; an argument that names none is the same for every part. Nothing has to cross between parts.
Inputs may be any that keep to these rules, and one draw needn't show every extreme that they name: `qk_gains`: positive gains.
All inputs are finite; a program needn't handle non-finite values.
Results may differ from a plain program's by a relative error of at most 0.014.
Values may be sent and summed in bfloat16 or wider, within the bound.
No kernel may reach another device: no remote copies, remote signals or barrier semaphores. Data moves between devices by JAX's collectives and lax.ppermute only.
A program may use at most 128 MiB of HBM per device.

v0:
```python
import math
import jax
import jax.numpy as jnp
from jax import lax
from jax.sharding import PartitionSpec as P

STEPS = 28
EPS = 1e-06
SHIFT_MU = 1.15
THETA = 10000.0


def extended(block, sides, width):
    for axis, dim in sides:
        count = lax.axis_size(axis)
        forward = [(i, i + 1) for i in range(count - 1)]
        backward = [(target, source) for source, target in forward]
        low = lax.ppermute(
            lax.slice_in_dim(block, block.shape[dim] - width, None, axis=dim), axis, forward
        )
        high = lax.ppermute(lax.slice_in_dim(block, 0, width, axis=dim), axis, backward)
        block = jnp.concatenate([low, block, high], axis=dim)
    return block


def modulate(hidden, mod_rows):
    values = hidden.astype(jnp.float32)
    mod_f = mod_rows.astype(jnp.float32)
    row_mean = jnp.mean(values, -1, keepdims=True)
    row_var = jnp.mean((values - row_mean) ** 2, -1, keepdims=True)
    normed = (values - row_mean) * lax.rsqrt(row_var + EPS)
    return (normed * (1.0 + mod_f[1]) + mod_f[0]).astype(jnp.bfloat16)


def rms_gain(values, gain_row):
    return values * lax.rsqrt(jnp.mean(values * values, -1, keepdims=True) + EPS) * gain_row


def rope_angles(row_pos, col_pos, head_dim):
    lead = head_dim // 16
    span = 7 * head_dim // 32
    freq = THETA ** (-jnp.arange(span, dtype=jnp.float32) / span)
    zero_part = jnp.zeros((row_pos.shape[0], lead), jnp.float32)
    return jnp.concatenate(
        [zero_part, row_pos[:, None] * freq[None], col_pos[:, None] * freq[None]], 1
    )


def apply_rope(values, angles):
    count, heads_n, head_dim = values.shape
    pairs = values.reshape(count, heads_n, head_dim // 2, 2)
    first = pairs[..., 0]
    second = pairs[..., 1]
    cosine = jnp.cos(angles)[:, None, :]
    sine = jnp.sin(angles)[:, None, :]
    turned = jnp.stack([first * cosine - second * sine, first * sine + second * cosine], -1)
    return turned.reshape(values.shape)


def split_heads(mixed, gain_q, gain_k, angles):
    head_dim = gain_q.shape[0]
    shaped = mixed.reshape(mixed.shape[0], 3, -1, head_dim)
    query = rms_gain(shaped[:, 0], gain_q)
    keyed = rms_gain(shaped[:, 1], gain_k)
    if angles is not None:
        query = apply_rope(query, angles)
        keyed = apply_rope(keyed, angles)
    return (
        query.astype(jnp.bfloat16),
        keyed.astype(jnp.bfloat16),
        shaped[:, 2].astype(jnp.bfloat16),
    )


def noise_level(tval):
    factor = math.exp(SHIFT_MU)
    return factor * tval / (factor * tval + 1.0 - tval)


def add_rows(normed, piece):
    flat_piece = piece.reshape(piece.shape[0], piece.shape[1] * piece.shape[2])
    return jnp.dot(normed, flat_piece, preferred_element_type=jnp.float32)


def per_device(
    img_hidden,
    txt_hidden,
    img_mod,
    txt_mod,
    img_qkv,
    txt_qkv,
    qk_gains,
    img_out_w,
    txt_out_w,
    final_mod,
    final_w,
    conv_w,
    latent,
    text_len,
    step_index,
):
    seq_count = lax.axis_size("seq")
    seq_at = lax.axis_index("seq")
    tp_at = lax.axis_index("tp")
    img_rows = img_hidden.shape[0]
    txt_rows = txt_hidden.shape[0]
    local_width = img_hidden.shape[1]
    img_full, txt_full = (
        lax.all_gather(img_hidden, "tp", axis=1, tiled=True),
        lax.all_gather(txt_hidden, "tp", axis=1, tiled=True),
    )
    full_width = img_full.shape[1]
    img_norm = modulate(img_full, img_mod)
    txt_norm = modulate(txt_full, txt_mod)
    img_mixed = add_rows(img_norm, lax.all_gather(img_qkv, "seq", axis=0, tiled=True))
    txt_norm_rows = lax.all_to_all(txt_norm, "seq", 1, 0, tiled=True)
    txt_mixed = lax.psum_scatter(
        add_rows(txt_norm_rows, txt_qkv), "seq", scatter_dimension=0, tiled=True
    )
    head_dim = qk_gains.shape[1]
    grid_side = latent.shape[0] * seq_count
    token_ids = seq_at * img_rows + jnp.arange(img_rows, dtype=jnp.int32)
    row_pos = (token_ids // grid_side).astype(jnp.float32)
    col_pos = (token_ids % grid_side).astype(jnp.float32)
    angles = rope_angles(row_pos, col_pos, head_dim)
    img_query, img_key, img_value = split_heads(img_mixed, qk_gains[0], qk_gains[1], angles)
    txt_query, txt_key, txt_value = split_heads(txt_mixed, qk_gains[2], qk_gains[3], None)
    local_len = txt_rows + img_rows
    heads_local = img_query.shape[1]
    queries = jnp.concatenate([txt_query, img_query], 0)
    keys_local = jnp.concatenate([txt_key, img_key], 0).reshape(local_len, heads_local * head_dim)
    values_local = jnp.concatenate([txt_value, img_value], 0).reshape(
        local_len, heads_local * head_dim
    )
    limit = text_len[0]
    score_scale = head_dim ** (-0.5)
    start_state = (
        jnp.full((heads_local, local_len), -1e30, jnp.float32),
        jnp.zeros((heads_local, local_len), jnp.float32),
        jnp.zeros((heads_local, local_len, head_dim), jnp.float32),
    )
    key_piece = lax.all_gather(keys_local, "seq", axis=0, tiled=True)
    value_piece = lax.all_gather(values_local, "seq", axis=0, tiled=True)
    blocks = key_piece.shape[0] // local_len

    def advance(block, state):
        peak, running, accum = state
        key_block = lax.dynamic_slice_in_dim(key_piece, block * local_len, local_len, 0).reshape(
            local_len, heads_local, head_dim
        )
        value_block = lax.dynamic_slice_in_dim(
            value_piece, block * local_len, local_len, 0
        ).reshape(local_len, heads_local, head_dim)
        within = jnp.arange(local_len, dtype=jnp.int32)
        text_pos = block * txt_rows + within
        usable = (within >= txt_rows) | (text_pos < limit)
        scores = (
            jnp.einsum("qhd,khd->hqk", queries, key_block, preferred_element_type=jnp.float32)
            * score_scale
        )
        scores = jnp.where(usable[None, None, :], scores, -1e30)
        new_peak = jnp.maximum(peak, jnp.max(scores, -1))
        rescale = jnp.exp(peak - new_peak)
        weights = jnp.exp(scores - new_peak[..., None])
        running = running * rescale + jnp.sum(weights, -1)
        accum = accum * rescale[..., None] + jnp.einsum(
            "hqk,khd->hqd",
            weights.astype(jnp.bfloat16),
            value_block,
            preferred_element_type=jnp.float32,
        )
        return (new_peak, running, accum)

    peak, running, accum = lax.fori_loop(0, blocks, advance, start_state)
    attn = (
        (accum / running[..., None])
        .astype(jnp.bfloat16)
        .transpose(1, 0, 2)
        .reshape(local_len, heads_local * head_dim)
    )
    txt_attn = attn[:txt_rows]
    img_attn = attn[txt_rows:]
    img_term = jnp.dot(
        img_attn,
        lax.all_gather(img_out_w, "seq", axis=1, tiled=True),
        preferred_element_type=jnp.float32,
    )
    txt_term = jnp.dot(
        lax.all_gather(txt_attn, "seq", axis=0, tiled=True),
        txt_out_w,
        preferred_element_type=jnp.float32,
    )
    txt_part = lax.psum_scatter(
        txt_term.astype(jnp.bfloat16).astype(jnp.float32), "tp", scatter_dimension=0, tiled=True
    )
    side = lax.axis_size("tp")
    swap = [(a * side + b, b * side + a) for a in range(side) for b in range(side)]
    txt_out = lax.ppermute(txt_part, ("seq", "tp"), swap)
    img_out = lax.psum_scatter(
        img_term.astype(jnp.bfloat16), "tp", scatter_dimension=1, tiled=True
    ).astype(jnp.float32)
    img_gate = lax.dynamic_slice_in_dim(
        img_mod.astype(jnp.float32)[2], tp_at * local_width, local_width
    )
    txt_gate = lax.dynamic_slice_in_dim(
        txt_mod.astype(jnp.float32)[2], tp_at * local_width, local_width
    )
    img_next = (img_hidden.astype(jnp.float32) + img_gate * img_out).astype(jnp.bfloat16)
    text_valid = seq_at * txt_rows + jnp.arange(txt_rows, dtype=jnp.int32) < limit
    txt_base = txt_hidden.astype(jnp.float32)
    txt_next = jnp.where(text_valid[:, None], txt_base + txt_gate * txt_out, txt_base).astype(
        jnp.bfloat16
    )
    shift_row = lax.dynamic_slice_in_dim(final_mod[0], tp_at * local_width, local_width)
    scale_row = lax.dynamic_slice_in_dim(final_mod[1], tp_at * local_width, local_width)
    final_shift = shift_row.astype(jnp.float32)
    final_scale = scale_row.astype(jnp.float32)
    weight_final = final_w.astype(jnp.float32)
    values = img_next.astype(jnp.float32)
    channels = final_w.shape[1]
    final_gain = 1.0 + final_scale
    high = lax.Precision.HIGHEST
    lifted = jnp.dot(values * final_gain, weight_final, precision=high)
    consts = jnp.stack(
        [
            jnp.dot(final_gain, weight_final, precision=high),
            jnp.dot(final_shift, weight_final, precision=high),
        ]
    )
    packed = jnp.concatenate(
        [
            jnp.concatenate(
                [lifted, jnp.sum(values, -1)[:, None], jnp.sum(values * values, -1)[:, None]], 1
            ),
            jnp.pad(consts, ((0, 0), (0, 2))),
        ],
        0,
    )
    packed = lax.psum(packed, "tp")
    lifted = packed[:img_rows, :channels]
    row_mean = packed[:img_rows, channels] / full_width
    row_var = packed[:img_rows, channels + 1] / full_width - row_mean * row_mean
    row_scale = lax.rsqrt(row_var + EPS)[:, None]
    patch = (
        row_scale * (lifted - row_mean[:, None] * packed[img_rows, :channels])
        + packed[img_rows + 1, :channels]
    )
    band_rows = latent.shape[0]
    patch_band = patch.astype(jnp.bfloat16).reshape(band_rows, grid_side * channels)
    rimmed = extended(patch_band, (("seq", 0),), 1)
    col_width = latent.shape[1] // channels
    framed = jnp.pad(rimmed.reshape(band_rows + 2, grid_side, channels), ((0, 0), (1, 1), (0, 0)))
    window = lax.dynamic_slice_in_dim(framed, tp_at * col_width, col_width + 2, 1)
    velocity = jnp.zeros((band_rows, col_width, channels), jnp.float32)
    for row_shift in range(3):
        for col_shift in range(3):
            velocity = velocity + jnp.einsum(
                "rci,io->rco",
                window[row_shift : row_shift + band_rows, col_shift : col_shift + col_width],
                conv_w[row_shift, col_shift],
                preferred_element_type=jnp.float32,
            )
    velocity_flat = velocity.reshape(band_rows, col_width * channels)
    step_f = step_index[0].astype(jnp.float32)
    t_now = 1.0 - step_f / STEPS
    t_after = 1.0 - (step_f + 1.0) / STEPS
    delta = noise_level(t_after) - noise_level(t_now)
    latent_next = latent + delta * velocity_flat
    denoised = latent - noise_level(t_now) * velocity_flat
    return (img_next, txt_next, velocity_flat, latent_next, denoised)


def solution(mesh):
    placed = (
        P(("req", "seq"), "tp"),
        P(("req", "seq"), "tp"),
        P("req", None),
        P("req", None),
        P("seq", None, "tp"),
        P("seq", None, "tp"),
        P(),
        P("tp", "seq"),
        P("tp", "seq"),
        P("req", None),
        P("tp", None),
        P(),
        P(("req", "seq"), "tp"),
        P("req"),
        P("req"),
    )
    return jax.shard_map(
        per_device,
        mesh=mesh,
        in_specs=placed,
        out_specs=(
            P(("req", "seq"), "tp"),
            P(("req", "seq"), "tp"),
            P(("req", "seq"), "tp"),
            P(("req", "seq"), "tp"),
            P(("req", "seq"), "tp"),
        ),
        check_vma=False,
    )
```

profile of v0, /device:TPU:24, one launch (start us, length us, event | category | flops | bytes accessed | tf_op | source)
XLA Modules:
  0.0 591.8 jit_solution(8181375661822205329)
XLA Ops:
  10.2 18.8 %all_gather.21 = bf16[64,3072]{1,0:T(8,128)(2,1)S(1)} all-gather(bf16[64,384]{1,0:T(8,128)(2,1)} %param.18), channel_id=1, replica_groups=mesh['req'=4,'seq'=8,'tp'=8] {'tp'}, dimensions={1}, use_global_device_ids=true | all-gather | bytes 442368 | tf_op jit(solution)/shard_map/all_gather | solution.py:110
  30.4 5.4 all-to-all-start
  38.3 4.1 all-to-all-done
  51.8 57.2 %reduce-scatter.6.cloned.1.call-done = f32[64,1152]{1,0:T(8,128)} async-done(((f32[512,1152]{1,0:T(8,128)}), f32[64,1152]{1,0:T(8,128)}) %reduce-scatter.6.cloned.1.call-update) | async-done | bytes 294928 | tf_op jit(solution)/shard_map/reduce_scatter | solution.py:117
  115.1 61.8 %all-gather.8.cloned.1.call-done = bf16[3072,3,384]{0,2,1:T(8,128)(2,1)} async-done(((bf16[384,3,384]{0,2,1:T(8,128)(2,1)}), bf16[3072,3,384]{0,2,1:T(8,128)(2,1)}) %all-gather.8.cloned.1.call-update) | async-done | bytes 7077904 | tf_op jit(solution)/shard_map/all_gather | solution.py:115
  176.9 6.4 %fusion.23 = f32[512,3,3,128]{0,3,2,1:T(8,128)S(1)} fusion(bf16[3,3,128,3072]{3,2,1,0:T(8,128)(2,1)} %bitcast.197, bf16[512,3072]{1,0:T(8,128)(2,1)S(1)} %copy-done.1, f32[3072]{0:T(1024)} %bitcast.192, f32[3072]{0:T(1024)S(1)} %bitcast.191, f32[512]{0:T(512)} %add_rsqrt_fusion.5, f32[512]{0:T(512)S(1)} %broadcast_multiply_fusion.2), kind=kOutput, calls=%fused_computation.34 | convolution fusion | flops 3633315840 | bytes 12611584 | tf_op jit(solution)/shard_map/dot_general | solution.py:82
  196.1 43.4 %all-gather.10.cloned.1.call-done = bf16[4608,384]{1,0:T(8,128)(2,1)} async-done(((bf16[576,384]{1,0:T(8,128)(2,1)}), bf16[4608,384]{1,0:T(8,128)(2,1)}) %all-gather.10.cloned.1.call-update) | async-done | bytes 3538960 | tf_op jit(solution)/shard_map/all_gather | solution.py:142
  239.5 50.3 %all-gather.12.cloned.1.call-done = bf16[4608,384]{1,0:T(8,128)(2,1)} async-done(((bf16[576,384]{1,0:T(8,128)(2,1)}), bf16[4608,384]{1,0:T(8,128)(2,1)}) %all-gather.12.cloned.1.call-update) | async-done | bytes 3538960 | tf_op jit(solution)/shard_map/all_gather | solution.py:143
  289.8 104.1 %while.18 = (s32[]{:T(128)}, f32[3,576]{1,0:T(4,128)S(1)}, f32[3,576]{1,0:T(4,128)}, f32[3,576,128]{2,1,0:T(8,128)S(1)}, s32[]{:T(128)}, /*index=5*/bf16[4608,38...) while((s32[]{:T(128)}, f32[3,576]{1,0:T(4,128)S(1)}, ...), condition=%wide.region_12.13_spmd.clone, body=%wide.region_9.12_spmd.clone.sunk | while | flops 521231040 | bytes 18747912 | solution.py:174
  298.6 4.1 fusion.135
  311.7 4.1 fusion.135
  324.7 4.2 fusion.135
  337.7 4.1 fusion.135
  350.7 4.1 fusion.135
  363.7 4.1 fusion.135
  376.7 4.1 fusion.135
  389.7 4.1 fusion.135
  396.7 3.6 convolution_convert_fusion
  403.4 31.2 %all_gather.27 = bf16[512,384]{1,0:T(8,128)(2,1)S(1)} all-gather(bf16[64,384]{1,0:T(8,128)(2,1)S(1)} %copy.129), channel_id=1, replica_groups=mesh['req'=4,'seq'=8,'tp'=8] {'seq'}, dimensions={0}, use_global_device_ids=true | all-gather | bytes 442368 | tf_op jit(solution)/shard_map/all_gather | solution.py:189
  437.2 18.4 %reduce-scatter.10.cloned.1.call-done = bf16[384,512]{1,0:T(8,128)(2,1)} async-done(((bf16[3072,512]{1,0:T(8,128)(2,1)}), bf16[384,512]{1,0:T(8,128)(2,1)}) %reduce-scatter.10.cloned.1.call-update) | async-done | bytes 393232
  460.6 34.9 %reduce-scatter.8.cloned.1.call-done = f32[64,384]{1,0:T(8,128)} async-done(((f32[512,384]{1,0:T(8,128)}), f32[64,384]{1,0:T(8,128)}) %reduce-scatter.8.cloned.1.call-update) | async-done | bytes 98320 | tf_op jit(solution)/shard_map/reduce_scatter | solution.py:193
  495.5 4.1 collective-permute-start
  499.6 69.3 %all-reduce.4.cloned.1.call-done = f32[514,66]{0,1:T(8,128)} async-done(((f32[514,66]{0,1:T(8,128)}), f32[514,66]{0,1:T(8,128)}) %all-reduce.4.cloned.1.call-update) | async-done | bytes 135712 | tf_op jit(solution)/shard_map/psum | solution.py:239
  574.6 3.4 collective-permute-start.2
  (281 shorter events, 128.3 us)
Async XLA Ops:
  8.0 426.6 %copy-start = (bf16[384,384]{1,0:T(8,128)(2,1)S(1)}, bf16[384,384]{1,0:T(8,128)(2,1)}, u32[]{:S(2)}) copy-start(bf16[384,384]{1,0:T(8,128)(2,1)} %param.25) | copy-start | bytes 884740
  30.4 14.8 %copy-start.8 = (bf16[384,3,384]{2,0,1:T(8,128)(2,1)S(1)}, bf16[384,3,384]{2,0,1:T(8,128)(2,1)}, u32[]{:S(2)}) copy-start(bf16[384,3,384]{2,0,1:T(8,128)(2,1)} %param.21) | copy-start | bytes 2654212
  30.4 11.9 %all-to-all-start = ((bf16[64,8,384]{2,0,1:T(8,128)(2,1)}), bf16[64,8,384]{2,0,1:T(8,128)(2,1)S(1)}, u32[]{:S(2)}, u32[]{:S(2)}) async-start(bf16[64,8,384]{2,0,1:T(8,128)(2,1)} %bitcast.155), calls=%async_computation | async-start | bytes 786432 | tf_op jit(solution)/shard_map/all_to_all | solution.py:116
  35.8 73.2 %reduce-scatter.6.cloned.1.call-start = ((), (), s32[]{:S(2)}) async-start(), calls=%async_computation.4 | async-start | bytes 2654208 | tf_op jit(solution)/shard_map/reduce_scatter | solution.py:117
  44.6 66.2 %all-gather.6.cloned.1.call-start = ((), (), s32[]{:S(2)}) async-start(), calls=%async_computation.5 | async-start | bytes 3538944 | tf_op jit(solution)/shard_map/all_gather | solution.py:109
  45.2 131.8 %all-gather.8.cloned.1.call-start = ((), (), s32[]{:S(2)}) async-start(), calls=%async_computation.6 | async-start | bytes 7962624 | tf_op jit(solution)/shard_map/all_gather | solution.py:115
  47.4 192.1 %all-gather.10.cloned.1.call-start = ((), (), s32[]{:S(2)}) async-start(), calls=%async_computation.7 | async-start | bytes 3981312 | tf_op jit(solution)/shard_map/all_gather | solution.py:142
  190.9 98.9 %all-gather.12.cloned.1.call-start = ((), (), s32[]{:S(2)}) async-start(), calls=%async_computation.8 | async-start | bytes 3981312 | tf_op jit(solution)/shard_map/all_gather | solution.py:143
  193.2 203.5 %all-gather.14.cloned.1.call-start = ((), (), s32[]{:S(2)}) async-start(), calls=%async_computation.9 | async-start | bytes 2654208 | tf_op jit(solution)/shard_map/all_gather | solution.py:185
  193.8 261.8 %reduce-scatter.10.cloned.1.call-start = ((), (), s32[]{:S(2)}) async-start(), calls=%async_computation.12 | async-start | bytes 3538944
  305.0 6.4 %copy-start.12 = (f32[3,576]{1,0:T(4,128)S(1)}, f32[3,576]{1,0:T(4,128)}, u32[]{:S(2)}) copy-start(f32[3,576]{1,0:T(4,128)} %get-tuple-element.355) | copy-start | bytes 20740 | tf_op jit(solution)/shard_map/while
  318.0 6.4 %copy-start.12 = (f32[3,576]{1,0:T(4,128)S(1)}, f32[3,576]{1,0:T(4,128)}, u32[]{:S(2)}) copy-start(f32[3,576]{1,0:T(4,128)} %get-tuple-element.355) | copy-start | bytes 20740 | tf_op jit(solution)/shard_map/while
  403.2 32.8 %copy-start.20 = (bf16[2,3072]{1,0:T(2,128)(2,1)S(1)}, bf16[2,3072]{1,0:T(2,128)(2,1)}, u32[]{:S(2)}) copy-start(bf16[2,3072]{1,0:T(2,128)(2,1)} %param.26) | copy-start | bytes 36868
  403.2 32.9 %copy-start.11 = (bf16[384,64]{0,1:T(8,128)(2,1)S(1)}, bf16[384,64]{0,1:T(8,128)(2,1)}, u32[]{:S(2)}) copy-start(bf16[384,64]{0,1:T(8,128)(2,1)} %param.27) | copy-start | bytes 147460
  403.2 53.7 %copy-start.6 = (bf16[512,384]{1,0:T(8,128)(2,1)S(1)}, bf16[512,384]{1,0:T(8,128)(2,1)}, u32[]{:S(2)}) copy-start(bf16[512,384]{1,0:T(8,128)(2,1)} %param.17) | copy-start | bytes 1179652
  403.2 174.8 %copy-start.14 = (bf16[64,384]{1,0:T(8,128)(2,1)S(1)}, bf16[64,384]{1,0:T(8,128)(2,1)}, u32[]{:S(2)}) copy-start(bf16[64,384]{1,0:T(8,128)(2,1)} %param.18) | copy-start | bytes 147460
  403.2 179.4 %copy-start.15 = (bf16[3,3,64,64]{3,2,1,0:T(8,128)(2,1)S(1)}, bf16[3,3,64,64]{3,2,1,0:T(8,128)(2,1)}, u32[]{:S(2)}) copy-start(bf16[3,3,64,64]{3,2,1,0:T(8,128)(2,1)} %param.28) | copy-start | bytes 221188
  403.2 180.6 %copy-start.21 = (f32[8,512]{1,0:T(8,128)S(1)}, f32[8,512]{1,0:T(8,128)}, u32[]{:S(2)}) copy-start(f32[8,512]{1,0:T(8,128)} %param.29) | copy-start | bytes 49156
  403.2 92.3 %reduce-scatter.8.cloned.1.call-start = ((), (), s32[]{:S(2)}) async-start(), calls=%async_computation.10 | async-start | bytes 884736 | tf_op jit(solution)/shard_map/reduce_scatter | solution.py:193
  435.9 132.9 %all-reduce.4.cloned.1.call-start = ((), (), s32[]{:S(2)}) async-start(), calls=%async_computation.11 | async-start | bytes 368640 | tf_op jit(solution)/shard_map/psum | solution.py:239
  457.1 127.3 %copy-start.7 = (bf16[512,384]{1,0:T(8,128)(2,1)}, bf16[512,384]{1,0:T(8,128)(2,1)S(1)}, u32[]{:S(2)}) copy-start(bf16[512,384]{1,0:T(8,128)(2,1)S(1)} %get-tuple-element.240) | copy-start | bytes 1179652
  495.5 82.5 %collective-permute-start = (f32[64,384]{1,0:T(8,128)}, f32[64,384]{1,0:T(8,128)S(1)}, u32[]{:S(2)}, u32[]{:S(2)}) collective-permute-start(f32[64,384]{1,0:T(8,128)} %reduce-scatter.8.cloned.1.call-done), channel_id=1, source_target_pairs={{0,0},{1,8},{2,16},{3,24},{4,32},{5,40},{6,48},{7,56},{8,1},{9,9},... | collective-permute-start | bytes 294920 | tf_op jit(solution)/shard_map/ppermute | solution.py:198
  572.0 6.9 %collective-permute-start.1 = (bf16[1,4096]{1,0:T(2,128)(2,1)S(1)}, bf16[1,4096]{1,0:T(2,128)(2,1)S(1)}, u32[]{:S(2)}, u32[]{:S(2)}) collective-permute-start(bf16[1,4096]{1,0:T(2,128)(2,1)S(1)} %slice.193), channel_id=1, source_target_pairs={{0,8},{8,16},{16,24},{24,32},{32,40},{40,48},{48,56},{1,9},{9,17},... | collective-permute-start | bytes 24584 | tf_op jit(solution)/shard_map/ppermute | solution.py:18
  574.6 7.7 %collective-permute-start.2 = (bf16[1,4096]{1,0:T(2,128)(2,1)S(1)}, bf16[1,4096]{1,0:T(2,128)(2,1)S(1)}, u32[]{:S(2)}, u32[]{:S(2)}) collective-permute-start(bf16[1,4096]{1,0:T(2,128)(2,1)S(1)} %slice.195), channel_id=1, source_target_pairs={{8,0},{16,8},{24,16},{32,24},{40,32},{48,40},{56,48},{9,1},{17,9},... | collective-permute-start | bytes 24584 | tf_op jit(solution)/shard_map/ppermute | solution.py:21
  (28 other events, 115.2 us)
Sparse Core Ops, SparseCore 0:
  44.7 64.2 reduce-scatter.5
  191.0 48.4 all-gather.9
  241.3 48.4 all-gather.11
  291.4 44.1 all-gather.13
Sparse Core Ops, SparseCore 1:
  46.9 50.9 all-gather.5
  99.5 77.4 all-gather.7
  403.3 52.3 reduce-scatter.9
  458.2 37.3 reduce-scatter.7
  498.3 70.5 all-reduce.3
where the time goes:
time: 594 us; the launch traced here: 592 us
  waiting for transfers between devices  344 us (58%)
  matrix products  73.2 us (12%)
  blocking collectives  50 us (8%)
  other arithmetic  49.9 us (8%)
  local copies, waits for them, and re-layouts  40.5 us (7%)
  between operations  17.5 us (3%)
  starting transfers between devices  16 us (3%)
    psum x1, waiting for transfers between devices, per_device(): packed = lax.psum(packed, 'tp')  69.3 us
    all_gather x1, waiting for transfers between devices, per_device(): lax.all_gather(img_qkv, 'seq', axis=0, tiled=True)  61.8 us
    reduce_scatter x1, waiting for transfers between devices, per_device(): lax.psum_scatter(add_rows(txt_norm_rows, txt_qkv), 'seq', scatter_dimensi...  57.2 us
    all_gather x1, waiting for transfers between devices, per_device(): value_piece = lax.all_gather(values_local, 'seq', axis=0, tiled=True)  50.3 us
    all_gather x1, waiting for transfers between devices, per_device(): key_piece = lax.all_gather(keys_local, 'seq', axis=0, tiled=True)  43.4 us
    reduce_scatter x1, waiting for transfers between devices, per_device(): lax.psum_scatter(txt_term.astype(jnp.bfloat16).astype(jnp.float32), 'tp',...  34.9 us
    dot_general x8, matrix products, advance(): jnp.einsum('hqk,khd->hqd', weights.astype(jnp.bfloat16), value_block, pre...  33 us
    all_gather x1, blocking collectives, per_device(): lax.all_gather(txt_attn, 'seq', axis=0, tiled=True)  31.2 us
  transfers between devices with their start and end apart: 13, of which 9 were waited for; matrix products, arithmetic and copies ran while one was open for 23% of the time, Pallas kernels for 0%

commit v1 on v0

--- a/solution.py
+++ b/solution.py
@@ -112,7 +112,12 @@
     full_width = img_full.shape[1]
     img_norm = modulate(img_full, img_mod)
     txt_norm = modulate(txt_full, txt_mod)
-    img_mixed = add_rows(img_norm, lax.all_gather(img_qkv, "seq", axis=0, tiled=True))
+    img_mixed = add_rows(
+        img_norm,
+        jnp.concatenate(
+            lax.all_to_all(jnp.stack([img_qkv] * lax.axis_size("seq")), "seq", 0, 0), axis=0
+        ),
+    )
     txt_norm_rows = lax.all_to_all(txt_norm, "seq", 1, 0, tiled=True)
     txt_mixed = lax.psum_scatter(
         add_rows(txt_norm_rows, txt_qkv), "seq", scatter_dimension=0, tiled=True

time: 594 us -> 603 us (1.015)
  local copies, waits for them, and re-layouts: 40.5 us -> 56.5 us
  waiting for transfers between devices: 344 us -> 331 us
  starting transfers between devices: 16 us -> 22.7 us
    all_gather x1 -> x0, waiting for transfers between devices: 61.8 us -> none  [per_device(): lax.all_gather(img_qkv, 'seq', axis=0, tiled=True)]
    reduce_scatter x1, waiting for transfers between devices: 57.2 us -> 92.8 us  [per_device(): lax.psum_scatter(add_rows(txt_norm_rows, txt_qkv), 'seq', scatter_dimensi...]
    all_to_all x0 -> x1, waiting for transfers between devices: none -> 15.8 us  [per_device(): lax.all_to_all(jnp.stack([img_qkv] * lax.axis_size('seq')), 'seq', 0, 0)]
    all_to_all x0 -> x1, local copies, waits for them, and re-layouts: none -> 7.23 us  [per_device(): lax.all_to_all(jnp.stack([img_qkv] * lax.axis_size('seq')), 'seq', 0, 0)]
    all_to_all x0 -> x1, starting transfers between devices: none -> 6.98 us  [per_device(): lax.all_to_all(jnp.stack([img_qkv] * lax.axis_size('seq')), 'seq', 0, 0)]
    unnamed x50 -> x55, local copies, waits for them, and re-layouts: 11.5 us -> 16.4 us
    unnamed x10 -> x9, waiting for transfers between devices: 19.6 us -> 19.4 us
where the time goes in v1:
time: 603 us; the launch traced here: 602 us
  waiting for transfers between devices  331 us (55%)
  matrix products  73 us (12%)
  local copies, waits for them, and re-layouts  56.5 us (9%)
  other arithmetic  50 us (8%)
  blocking collectives  50 us (8%)
  starting transfers between devices  22.7 us (4%)
  between operations  17.6 us (3%)
    reduce_scatter x1, waiting for transfers between devices, per_device(): lax.psum_scatter(add_rows(txt_norm_rows, txt_qkv), 'seq', scatter_dimensi...  92.8 us
    psum x1, waiting for transfers between devices, per_device(): packed = lax.psum(packed, 'tp')  69.2 us
    all_gather x1, waiting for transfers between devices, per_device(): value_piece = lax.all_gather(values_local, 'seq', axis=0, tiled=True)  50.3 us
    all_gather x1, waiting for transfers between devices, per_device(): key_piece = lax.all_gather(keys_local, 'seq', axis=0, tiled=True)  41.3 us
    reduce_scatter x1, waiting for transfers between devices, per_device(): lax.psum_scatter(txt_term.astype(jnp.bfloat16).astype(jnp.float32), 'tp',...  34.9 us
    dot_general x8, matrix products, advance(): jnp.einsum('hqk,khd->hqd', weights.astype(jnp.bfloat16), value_block, pre...  32.8 us
    all_gather x1, blocking collectives, per_device(): lax.all_gather(txt_attn, 'seq', axis=0, tiled=True)  31.2 us
    reduce_sum x8, other arithmetic, advance(): running = running * rescale + jnp.sum(weights, -1)  26 us
  transfers between devices with their start and end apart: 13, of which 9 were waited for; matrix products, arithmetic and copies ran while one was open for 23% of the time, Pallas kernels for 0%

profile of v1, /device:TPU:24, one launch (start us, length us, event | category | flops | bytes accessed | tf_op | source)
XLA Modules:
  0.0 601.6 jit_solution(7077696169847333164)
XLA Ops:
  10.2 18.8 %all_gather.18 = bf16[64,3072]{1,0:T(8,128)(2,1)S(1)} all-gather(bf16[64,384]{1,0:T(8,128)(2,1)} %param.18), channel_id=1, replica_groups=mesh['req'=4,'seq'=8,'tp'=8] {'tp'}, dimensions={1}, use_global_device_ids=true | all-gather | bytes 442368 | tf_op jit(solution)/shard_map/all_gather | solution.py:110
  30.4 5.2 all-to-all-start
  46.2 7.0 %all-to-all-start.1 = ((bf16[8,384,3,384]{1,3,2,0:T(8,128)(2,1)}), bf16[8,384,3,384]{1,3,2,0:T(8,128)(2,1)}, u32[]{:S(2)}, u32[]{:S(2)}) async-start(bf16[8,384,3,384]{1,3,2,0:T(8,128)(2,1)} %stack.14), calls=%async_computation.2 | async-start | bytes 14155776 | tf_op jit(solution)/shard_map/all_to_all | solution.py:118
  62.7 92.8 %reduce-scatter.6.cloned.1.call-done = f32[64,1152]{1,0:T(8,128)} async-done(((f32[512,1152]{1,0:T(8,128)}), f32[64,1152]{1,0:T(8,128)}) %reduce-scatter.6.cloned.1.call-update) | async-done | bytes 294928 | tf_op jit(solution)/shard_map/reduce_scatter | solution.py:122
  161.7 15.8 %all-to-all-done.1 = bf16[8,384,3,384]{1,3,2,0:T(8,128)(2,1)} async-done(((bf16[8,384,3,384]{1,3,2,0:T(8,128)(2,1)}), bf16[8,384,3,384]{1,3,2,0:T(8,128)(2,1)}, u32[]{:S(2)}, u32[]{:S(2)}) %all-to-all-start.1) | async-done | bytes 7077920 | tf_op jit(solution)/shard_map/all_to_all | solution.py:118
  177.5 7.2 %copy.132 = bf16[8,384,3,384]{1,0,3,2:T(8,128)(2,1)S(1)} copy(bf16[8,384,3,384]{1,3,2,0:T(8,128)(2,1)} %all-to-all-done.1) | data formatting | bytes 14155776 | tf_op jit(solution)/shard_map/all_to_all | solution.py:118
  184.8 4.7 copy.161
  189.4 6.4 %fusion.23 = f32[512,3,3,128]{0,3,2,1:T(8,128)S(1)} fusion(bf16[3,3,128,3072]{3,2,1,0:T(8,128)(2,1)} %bitcast.182, bf16[512,3072]{1,0:T(8,128)(2,1)S(1)} %copy-done.1, f32[3072]{0:T(1024)S(1)} %bitcast.198, f32[3072]{0:T(1024)S(1)} %bitcast.197, f32[512]{0:T(512)S(1)} %copy-done.25, f32[512]{0:T(512)S(1)} %broadcast_multiply_fusion.2), kind=kOutput, calls=%fused_computation.34 | convolution fusion | flops 3633315840 | bytes 12611584 | tf_op jit(solution)/shard_map/dot_general | solution.py:82
  208.4 41.3 %all-gather.7.cloned.1.call-done = bf16[4608,384]{1,0:T(8,128)(2,1)} async-done(((bf16[576,384]{1,0:T(8,128)(2,1)}), bf16[4608,384]{1,0:T(8,128)(2,1)}) %all-gather.7.cloned.1.call-update) | async-done | bytes 3538960 | tf_op jit(solution)/shard_map/all_gather | solution.py:147
  249.7 50.3 %all-gather.9.cloned.1.call-done = bf16[4608,384]{1,0:T(8,128)(2,1)} async-done(((bf16[576,384]{1,0:T(8,128)(2,1)}), bf16[4608,384]{1,0:T(8,128)(2,1)}) %all-gather.9.cloned.1.call-update) | async-done | bytes 3538960 | tf_op jit(solution)/shard_map/all_gather | solution.py:148
  300.0 103.9 %while.18 = (s32[]{:T(128)}, f32[3,576]{1,0:T(4,128)S(1)}, f32[3,576]{1,0:T(4,128)}, f32[3,576,128]{2,1,0:T(8,128)S(1)}, s32[]{:T(128)}, /*index=5*/bf16[4608,38...) while((s32[]{:T(128)}, f32[3,576]{1,0:T(4,128)S(1)}, ...), condition=%wide.region_12.13_spmd.clone, body=%wide.region_9.12_spmd.clone.sunk | while | flops 521231040 | bytes 18747920 | solution.py:179
  308.9 4.1 fusion.135
  321.9 4.1 fusion.135
  334.9 4.1 fusion.135
  347.9 4.1 fusion.135
  360.9 4.1 fusion.135
  373.9 4.1 fusion.135
  386.9 4.1 fusion.135
  399.8 4.1 fusion.135
  413.5 31.2 %all_gather.23 = bf16[512,384]{1,0:T(8,128)(2,1)S(1)} all-gather(bf16[64,384]{1,0:T(8,128)(2,1)S(1)} %copy.152), channel_id=1, replica_groups=mesh['req'=4,'seq'=8,'tp'=8] {'seq'}, dimensions={0}, use_global_device_ids=true | all-gather | bytes 442368 | tf_op jit(solution)/shard_map/all_gather | solution.py:194
  447.2 18.3 %reduce-scatter.10.cloned.1.call-done = bf16[384,512]{1,0:T(8,128)(2,1)} async-done(((bf16[3072,512]{1,0:T(8,128)(2,1)}), bf16[384,512]{1,0:T(8,128)(2,1)}) %reduce-scatter.10.cloned.1.call-update) | async-done | bytes 393232
  470.5 34.9 %reduce-scatter.8.cloned.1.call-done = f32[64,384]{1,0:T(8,128)} async-done(((f32[512,384]{1,0:T(8,128)}), f32[64,384]{1,0:T(8,128)}) %reduce-scatter.8.cloned.1.call-update) | async-done | bytes 98320 | tf_op jit(solution)/shard_map/reduce_scatter | solution.py:198
  505.4 4.1 collective-permute-start
  509.5 69.2 %all-reduce.4.cloned.1.call-done = f32[514,66]{0,1:T(8,128)} async-done(((f32[514,66]{0,1:T(8,128)}), f32[514,66]{0,1:T(8,128)}) %all-reduce.4.cloned.1.call-update) | async-done | bytes 135712 | tf_op jit(solution)/shard_map/psum | solution.py:244
  (287 shorter events, 143.3 us)
Async XLA Ops:
  8.0 436.7 %copy-start = (bf16[384,384]{1,0:T(8,128)(2,1)S(1)}, bf16[384,384]{1,0:T(8,128)(2,1)}, u32[]{:S(2)}) copy-start(bf16[384,384]{1,0:T(8,128)(2,1)} %param.25) | copy-start | bytes 884740
  30.4 11.8 %all-to-all-start = ((bf16[64,8,384]{2,0,1:T(8,128)(2,1)}), bf16[64,8,384]{2,0,1:T(8,128)(2,1)S(1)}, u32[]{:S(2)}, u32[]{:S(2)}) async-start(bf16[64,8,384]{2,0,1:T(8,128)(2,1)} %bitcast.159), calls=%async_computation | async-start | bytes 786432 | tf_op jit(solution)/shard_map/all_to_all | solution.py:121
  46.2 7.0 %copy-start.8 = (bf16[384,3,384]{2,0,1:T(8,128)(2,1)S(1)}, bf16[384,3,384]{2,0,1:T(8,128)(2,1)}, u32[]{:S(2)}) copy-start(bf16[384,3,384]{2,0,1:T(8,128)(2,1)} %param.22) | copy-start | bytes 2654212
  46.2 131.3 %all-to-all-start.1 = ((bf16[8,384,3,384]{1,3,2,0:T(8,128)(2,1)}), bf16[8,384,3,384]{1,3,2,0:T(8,128)(2,1)}, u32[]{:S(2)}, u32[]{:S(2)}) async-start(bf16[8,384,3,384]{1,3,2,0:T(8,128)(2,1)} %stack.14), calls=%async_computation.2 | async-start | bytes 14155776 | tf_op jit(solution)/shard_map/all_to_all | solution.py:118
  53.2 102.3 %reduce-scatter.6.cloned.1.call-start = ((), (), s32[]{:S(2)}) async-start(), calls=%async_computation.5 | async-start | bytes 2654208 | tf_op jit(solution)/shard_map/reduce_scatter | solution.py:122
  57.8 99.5 %all-gather.5.cloned.1.call-start = ((), (), s32[]{:S(2)}) async-start(), calls=%async_computation.6 | async-start | bytes 3538944 | tf_op jit(solution)/shard_map/all_gather | solution.py:109
  58.4 191.3 %all-gather.7.cloned.1.call-start = ((), (), s32[]{:S(2)}) async-start(), calls=%async_computation.7 | async-start | bytes 3981312 | tf_op jit(solution)/shard_map/all_gather | solution.py:147
  203.4 96.7 %all-gather.9.cloned.1.call-start = ((), (), s32[]{:S(2)}) async-start(), calls=%async_computation.8 | async-start | bytes 3981312 | tf_op jit(solution)/shard_map/all_gather | solution.py:148
  205.7 201.1 %all-gather.11.cloned.1.call-start = ((), (), s32[]{:S(2)}) async-start(), calls=%async_computation.9 | async-start | bytes 2654208 | tf_op jit(solution)/shard_map/all_gather | solution.py:190
  206.3 259.2 %reduce-scatter.10.cloned.1.call-start = ((), (), s32[]{:S(2)}) async-start(), calls=%async_computation.12 | async-start | bytes 3538944
  315.2 6.4 %copy-start.12 = (f32[3,576]{1,0:T(4,128)S(1)}, f32[3,576]{1,0:T(4,128)}, u32[]{:S(2)}) copy-start(f32[3,576]{1,0:T(4,128)} %get-tuple-element.363) | copy-start | bytes 20740 | tf_op jit(solution)/shard_map/while
  328.2 6.4 %copy-start.12 = (f32[3,576]{1,0:T(4,128)S(1)}, f32[3,576]{1,0:T(4,128)}, u32[]{:S(2)}) copy-start(f32[3,576]{1,0:T(4,128)} %get-tuple-element.363) | copy-start | bytes 20740 | tf_op jit(solution)/shard_map/while
  413.3 32.8 %copy-start.20 = (bf16[2,3072]{1,0:T(2,128)(2,1)S(1)}, bf16[2,3072]{1,0:T(2,128)(2,1)}, u32[]{:S(2)}) copy-start(bf16[2,3072]{1,0:T(2,128)(2,1)} %param.26) | copy-start | bytes 36868
  413.3 32.8 %copy-start.11 = (bf16[384,64]{0,1:T(8,128)(2,1)S(1)}, bf16[384,64]{0,1:T(8,128)(2,1)}, u32[]{:S(2)}) copy-start(bf16[384,64]{0,1:T(8,128)(2,1)} %param.27) | copy-start | bytes 147460
  413.3 53.5 %copy-start.6 = (bf16[512,384]{1,0:T(8,128)(2,1)S(1)}, bf16[512,384]{1,0:T(8,128)(2,1)}, u32[]{:S(2)}) copy-start(bf16[512,384]{1,0:T(8,128)(2,1)} %param.17) | copy-start | bytes 1179652
  413.3 174.6 %copy-start.14 = (bf16[64,384]{1,0:T(8,128)(2,1)S(1)}, bf16[64,384]{1,0:T(8,128)(2,1)}, u32[]{:S(2)}) copy-start(bf16[64,384]{1,0:T(8,128)(2,1)} %param.18) | copy-start | bytes 147460
  413.3 179.1 %copy-start.15 = (bf16[3,3,64,64]{3,2,1,0:T(8,128)(2,1)S(1)}, bf16[3,3,64,64]{3,2,1,0:T(8,128)(2,1)}, u32[]{:S(2)}) copy-start(bf16[3,3,64,64]{3,2,1,0:T(8,128)(2,1)} %param.28) | copy-start | bytes 221188
  413.3 180.3 %copy-start.21 = (f32[8,512]{1,0:T(8,128)S(1)}, f32[8,512]{1,0:T(8,128)}, u32[]{:S(2)}) copy-start(f32[8,512]{1,0:T(8,128)} %param.29) | copy-start | bytes 49156
  413.3 92.1 %reduce-scatter.8.cloned.1.call-start = ((), (), s32[]{:S(2)}) async-start(), calls=%async_computation.10 | async-start | bytes 884736 | tf_op jit(solution)/shard_map/reduce_scatter | solution.py:198
  446.0 132.7 %all-reduce.4.cloned.1.call-start = ((), (), s32[]{:S(2)}) async-start(), calls=%async_computation.11 | async-start | bytes 368640 | tf_op jit(solution)/shard_map/psum | solution.py:244
  467.1 127.2 %copy-start.7 = (bf16[512,384]{1,0:T(8,128)(2,1)}, bf16[512,384]{1,0:T(8,128)(2,1)S(1)}, u32[]{:S(2)}) copy-start(bf16[512,384]{1,0:T(8,128)(2,1)S(1)} %get-tuple-element.248) | copy-start | bytes 1179652
  505.4 82.5 %collective-permute-start = (f32[64,384]{1,0:T(8,128)}, f32[64,384]{1,0:T(8,128)S(1)}, u32[]{:S(2)}, u32[]{:S(2)}) collective-permute-start(f32[64,384]{1,0:T(8,128)} %reduce-scatter.8.cloned.1.call-done), channel_id=1, source_target_pairs={{0,0},{1,8},{2,16},{3,24},{4,32},{5,40},{6,48},{7,56},{8,1},{9,9},... | collective-permute-start | bytes 294920 | tf_op jit(solution)/shard_map/ppermute | solution.py:203
  581.8 6.9 %collective-permute-start.1 = (bf16[1,4096]{1,0:T(2,128)(2,1)S(1)}, bf16[1,4096]{1,0:T(2,128)(2,1)S(1)}, u32[]{:S(2)}, u32[]{:S(2)}) collective-permute-start(bf16[1,4096]{1,0:T(2,128)(2,1)S(1)} %slice.193), channel_id=1, source_target_pairs={{0,8},{8,16},{16,24},{24,32},{32,40},{40,48},{48,56},{1,9},{9,17},... | collective-permute-start | bytes 24584 | tf_op jit(solution)/shard_map/ppermute | solution.py:18
  584.5 7.7 %collective-permute-start.2 = (bf16[1,4096]{1,0:T(2,128)(2,1)S(1)}, bf16[1,4096]{1,0:T(2,128)(2,1)S(1)}, u32[]{:S(2)}, u32[]{:S(2)}) collective-permute-start(bf16[1,4096]{1,0:T(2,128)(2,1)S(1)} %slice.195), channel_id=1, source_target_pairs={{8,0},{16,8},{24,16},{32,24},{40,32},{48,40},{56,48},{9,1},{17,9},... | collective-permute-start | bytes 24584 | tf_op jit(solution)/shard_map/ppermute | solution.py:21
  (30 other events, 124.6 us)
Sparse Core Ops, SparseCore 0:
  58.0 97.4 reduce-scatter.5
  203.5 46.1 all-gather.6
  251.5 48.4 all-gather.8
  301.7 44.1 all-gather.10
Sparse Core Ops, SparseCore 1:
  60.2 74.2 all-gather.4
  413.4 52.1 reduce-scatter.9
  467.9 37.4 reduce-scatter.7
  508.2 70.4 all-reduce.3
